TPU v7x, 256 devices: a whole 4x4x8 slice. The times are simulated.
256 devices in a mesh: grp: 4 (over y), ex: 8 (over x, core), tp: 8 (over z).
Axes of the slice: x: 4, y: 4, z: 8, core: 2. Of those that a mesh axis runs over, the one named last changes fastest.
Arguments:
- residual: bfloat16 [512, 2, 6144], P(('grp', 'ex'), None, 'tp'), may hold values from -34 to 34
- query_new: bfloat16 [512, 2, 6144], P(('grp', 'ex'), None, 'tp'), may hold values from -5 to 5
- key_new: bfloat16 [512, 2, 1024], P(('grp', 'ex'), None, 'tp'), may hold values from -8 to 8
- value_new: bfloat16 [512, 2, 1024], P(('grp', 'ex'), None, 'tp'), may hold values from -12 to 12
- key_cache: bfloat16 [512, 8, 512, 128], P(('grp', 'ex'), 'tp'), may hold values from -5 to 5
- value_cache: bfloat16 [512, 8, 512, 128], P(('grp', 'ex'), 'tp'), may hold values from -12 to 12
- lengths: int32 [512], P(('grp', 'ex')), may hold values from 128 to 512, as said below
- norm_gain: bfloat16 [6144], P('tp'), may hold values from 0.099609375 to 1.8984375
- router: float32 [6144, 8], P('tp'), may hold values from -0.078125 to 0.078125
- routes: int32 [512, 2, 2], P(('grp', 'ex')), may hold values from 0 to 7, all different within a row; in each aligned block of 32 rows (0 to 31, 32 to 63, ..., all dimensions but the last counted through in order) at most 16 rows name the same one
- w_gate: bfloat16 [8, 6144, 8192], P('ex', None, ('grp', 'tp')), may hold values from -0.078125 to 0.078125
- w_up: bfloat16 [8, 6144, 8192], P('ex', None, ('grp', 'tp')), may hold values from -0.078125 to 0.078125
- w_down: bfloat16 [8, 8192, 6144], P('ex', ('grp', 'tp')), may hold values from -0.125 to 0.125
Outputs:
- attended: bfloat16 [512, 2, 6144], P(('grp', 'ex'), None, 'tp')
- expert_mix: bfloat16 [512, 2, 6144], P(('grp', 'ex'), None, 'tp')
Inputs may be any that keep to these rules, and one draw needn't show every extreme that they name: `routes`: over the rows of one device (aligned blocks of 32 rows, environments then steps) no expert is named more than 16 times, and in some blocks one is named exactly 16 times; a row's two experts differ. `lengths`: some environment's cache is full.
All inputs are finite; a program needn't handle non-finite values.
Results may differ from a plain program's by a relative error of at most 0.023.
Values may be sent and summed in bfloat16 or wider, within the bound.
No kernel may reach another device: no remote copies, remote signals or barrier semaphores. Data moves between devices by JAX's collectives and lax.ppermute only.
A program may use at most 128 MiB of HBM per device.

v0:
```python
import jax
import jax.numpy as jnp
from jax import lax
from jax.sharding import PartitionSpec as P

CAP = 16


def attend(query_new, key_new, value_new, key_cache, value_cache, lengths):
    env_count, step_count, feature_count = query_new.shape
    kv_count = key_cache.shape[1]
    context = key_cache.shape[2]
    head_dim = key_cache.shape[3]
    group_size = feature_count // (kv_count * head_dim)
    queries = query_new.reshape(env_count, step_count, kv_count, group_size, head_dim)
    keys_now = key_new.reshape(env_count, step_count, kv_count, head_dim)
    values_now = value_new.reshape(env_count, step_count, kv_count, head_dim)
    score_scale = head_dim ** (-0.5)
    cached = (
        jnp.einsum("eskgd,ekcd->eskgc", queries, key_cache, preferred_element_type=jnp.float32)
        * score_scale
    )
    fresh_scores = (
        jnp.einsum("eskgd,etkd->eskgt", queries, keys_now, preferred_element_type=jnp.float32)
        * score_scale
    )
    valid_mask = (lax.broadcasted_iota(jnp.int32, (env_count, context), 1) < lengths[:, None])[
        :, None, None, None, :
    ]
    causal = (
        lax.broadcasted_iota(jnp.int32, (step_count, step_count), 1)
        <= lax.broadcasted_iota(jnp.int32, (step_count, step_count), 0)
    )[None, :, None, None, :]
    cached = jnp.where(valid_mask, cached, -1e30)
    fresh_scores = jnp.where(causal, fresh_scores, -1e30)
    row_top = jnp.maximum(jnp.max(cached, -1), jnp.max(fresh_scores, -1))[..., None]
    weight_cached = jnp.where(valid_mask, jnp.exp(cached - row_top), 0.0)
    weight_fresh = jnp.where(causal, jnp.exp(fresh_scores - row_top), 0.0)
    row_total = (jnp.sum(weight_cached, -1) + jnp.sum(weight_fresh, -1))[..., None]
    probs_cached = (weight_cached / row_total).astype(jnp.bfloat16)
    probs_fresh = (weight_fresh / row_total).astype(jnp.bfloat16)
    heads_out = jnp.einsum(
        "eskgc,ekcd->eskgd", probs_cached, value_cache, preferred_element_type=jnp.float32
    )
    heads_out = heads_out + jnp.einsum(
        "eskgt,etkd->eskgd", probs_fresh, values_now, preferred_element_type=jnp.float32
    )
    return heads_out.reshape(env_count, step_count, feature_count)


def add_group(totals, addition, group_at):
    current = lax.dynamic_slice_in_dim(totals, group_at, 1, 1)
    return lax.dynamic_update_slice_in_dim(totals, current + addition[:, None], group_at, 1)


def per_device(
    residual,
    query_new,
    key_new,
    value_new,
    key_cache,
    value_cache,
    lengths,
    norm_gain,
    router,
    routes,
    w_gate,
    w_up,
    w_down,
):
    env_count, step_count, slice_width = residual.shape
    local_experts, width, hidden_local = w_gate.shape
    experts = router.shape[1]
    topk = routes.shape[2]
    group_count = lax.axis_size("grp")
    tensor_count = lax.axis_size("tp")
    owner_count = lax.axis_size("ex")
    row_count = env_count * step_count
    state = residual.astype(jnp.float32) + attend(
        query_new, key_new, value_new, key_cache, value_cache, lengths
    )
    attended = state.astype(jnp.bfloat16)
    squares = jnp.sum(state * state, -1)
    scaled = state * norm_gain.astype(jnp.float32)
    partial_logits = jnp.einsum("esd,dx->esx", scaled, router, precision=lax.Precision.HIGHEST)
    squares, logits = lax.psum((squares, partial_logits), "tp")
    root_mean = jnp.sqrt(squares / width + 1e-05)[..., None]
    logits = logits / root_mean
    normed = (scaled / root_mean).astype(jnp.bfloat16)
    expert_ids = lax.broadcasted_iota(jnp.int32, (1, 1, 1, experts), 3)
    picked_logits = jnp.sum(
        jnp.where(routes[..., None] == expert_ids, logits[:, :, None, :], 0.0), -1
    )
    first_gate = 1.0 / (1.0 + jnp.exp(picked_logits[..., 1] - picked_logits[..., 0]))
    second_gate = 1.0 - first_gate
    flat_routes = routes.reshape(row_count * topk)
    expert_hits = (flat_routes[:, None] == lax.broadcasted_iota(jnp.int32, (1, experts), 1)).astype(
        jnp.int32
    )
    earlier = jnp.cumsum(expert_hits, axis=0) - expert_hits
    slot_ids = jnp.sum(earlier * expert_hits, axis=1)
    targets = flat_routes * CAP + slot_ids
    slot_table = lax.broadcasted_iota(jnp.int32, (1, experts * CAP), 1)
    placed = (
        (targets[:, None] == slot_table)
        .astype(jnp.bfloat16)
        .reshape(row_count, topk, experts * CAP)
    )
    sender = jnp.sum(placed, axis=1)
    gate_init = jnp.zeros((local_experts, group_count, owner_count, CAP, hidden_local), jnp.float32)
    packed = jnp.einsum(
        "rs,rd->sd",
        sender,
        normed.reshape(row_count, slice_width),
        preferred_element_type=jnp.float32,
    )
    outgoing = packed.astype(jnp.bfloat16).reshape(experts, CAP, slice_width)
    received = lax.all_to_all(outgoing, "ex", split_axis=0, concat_axis=0, tiled=True)
    received = received.reshape(1, owner_count, local_experts, CAP, slice_width)
    pieces = lax.all_gather(received, ("grp", "tp"), axis=0, tiled=True)

    def add_block(position, running):
        block = lax.dynamic_index_in_dim(pieces, position, 0, keepdims=False)
        group_at = position // tensor_count
        column_at = position % tensor_count
        gate_rows = lax.dynamic_slice_in_dim(w_gate, column_at * slice_width, slice_width, 1)
        up_rows = lax.dynamic_slice_in_dim(w_up, column_at * slice_width, slice_width, 1)
        gate_add = jnp.einsum(
            "ajcd,jdf->jacf", block, gate_rows, preferred_element_type=jnp.float32
        )
        up_add = jnp.einsum("ajcd,jdf->jacf", block, up_rows, preferred_element_type=jnp.float32)
        return (add_group(running[0], gate_add, group_at), add_group(running[1], up_add, group_at))

    gate_sums, up_sums = lax.fori_loop(0, pieces.shape[0], add_block, (gate_init, gate_init))
    hidden = (jax.nn.silu(gate_sums) * up_sums).astype(jnp.bfloat16)
    down_split = w_down.reshape(local_experts, hidden_local, tensor_count, slice_width)
    down_terms = jnp.einsum(
        "jgacf,jftd->gtajcd", hidden, down_split, preferred_element_type=jnp.float32
    )
    down_terms = down_terms.reshape(
        group_count * tensor_count, owner_count, local_experts, CAP, slice_width
    )
    summed = lax.psum_scatter(
        down_terms.astype(jnp.bfloat16), ("grp", "tp"), scatter_dimension=0, tiled=True
    ).astype(jnp.float32)
    returned = lax.all_to_all(
        summed[0].astype(jnp.bfloat16), "ex", split_axis=0, concat_axis=0, tiled=True
    )
    returned = returned.reshape(experts * CAP, slice_width)
    picked_rows = jnp.einsum("rks,sd->rkd", placed, returned, preferred_element_type=jnp.float32)
    picked_rows = picked_rows.reshape(env_count, step_count, topk, slice_width)
    expert_mix = (
        first_gate[..., None] * picked_rows[:, :, 0] + second_gate[..., None] * picked_rows[:, :, 1]
    )
    return (attended, expert_mix.astype(jnp.bfloat16))


def solution(mesh):
    return jax.shard_map(
        per_device,
        mesh=mesh,
        in_specs=(
            P(("grp", "ex"), None, "tp"),
            P(("grp", "ex"), None, "tp"),
            P(("grp", "ex"), None, "tp"),
            P(("grp", "ex"), None, "tp"),
            P(("grp", "ex"), "tp", None, None),
            P(("grp", "ex"), "tp", None, None),
            P(("grp", "ex")),
            P("tp"),
            P("tp", None),
            P(("grp", "ex"), None, None),
            P("ex", None, ("grp", "tp")),
            P("ex", None, ("grp", "tp")),
            P("ex", ("grp", "tp"), None),
        ),
        out_specs=(P(("grp", "ex"), None, "tp"), P(("grp", "ex"), None, "tp")),
        check_vma=False,
    )
```

profile of v0, /device:TPU:1, one launch (start us, length us, event | category | flops | bytes accessed | tf_op | source)
XLA Modules:
  0.0 468.4 jit_solution(13371950069832483066)
XLA Ops:
  14.4 17.7 %all-reduce = (f32[16,2]{0,1:T(2,128)S(1)}, f32[16,2,8]{0,2,1:T(8,128)S(1)}) all-reduce(f32[16,2]{0,1:T(2,128)S(1)} %multiply_reduce_fusion, f32[16,2,8]{0,2,1:T(8,128)S(1)} %fusion.49), channel_id=1, replica_groups=mesh['grp'=4,'ex'=8,'tp'=8] {'tp'}, use_global_device_ids=true, to_apply=%region_6.7 | all-reduce | flops 288 | bytes 2304 | tf_op jit(solution)/shard_map/psum | solution.py:86
  33.5 14.3 %all_to_all.10 = bf16[8,16,768]{2,1,0:T(8,128)(2,1)} all-to-all(bf16[8,16,768]{2,1,0:T(8,128)(2,1)S(1)} %bitcast.169), channel_id=1, replica_groups=mesh['grp'=4,'ex'=8,'tp'=8] {'ex'}, dimensions={0} | all-to-all | bytes 393216 | tf_op jit(solution)/shard_map/all_to_all | solution.py:118
  47.9 4.5 copy.111
  52.4 79.5 %all-gather.3.cloned.1.call-done = bf16[256,16,768]{2,1,0:T(8,128)(2,1)} async-done(((bf16[8,16,768]{2,1,0:T(8,128)(2,1)}), bf16[256,16,768]{2,1,0:T(8,128)(2,1)}) %all-gather.3.cloned.1.call-update) | async-done | bytes 6291472 | tf_op jit(solution)/shard_map/all_gather | solution.py:120
  132.0 86.3 %while.17 = (s32[]{:T(128)}, f32[1,4,8,16,256]{4,3,2,1,0:T(8,128)S(1)}, f32[1,4,8,16,256]{4,3,2,1,0:T(8,128)S(1)}, bf16[32,8,1,16,768]{4,3,1,2,0:T(8,128)(2,1)},...) while((s32[]{:T(128)}, ...), condition=%wide.region_12.13_spmd, body=%wide.region_11.12_spmd.sunk | while | flops 100728848 | bytes 1704304 | solution.py:134
  133.4 1.3 fusion.86
  134.8 1.3 fusion.85
  136.1 1.3 fusion.86
  138.8 1.3 fusion.86
  141.5 1.3 fusion.86
  142.9 1.3 fusion.85
  144.2 1.3 fusion.86
  146.9 1.3 fusion.86
  149.6 1.3 fusion.86
  150.9 1.3 fusion.85
  152.3 1.3 fusion.86
  155.0 1.3 fusion.86
  157.7 1.3 fusion.86
  159.0 1.3 fusion.85
  160.4 1.3 fusion.86
  163.1 1.3 fusion.86
  165.8 1.3 fusion.86
  167.1 1.3 fusion.85
  168.5 1.3 fusion.86
  171.2 1.3 fusion.86
  173.9 1.3 fusion.86
  175.2 1.3 fusion.85
  176.6 1.3 fusion.86
  181.9 1.3 fusion.86
  183.3 1.3 fusion.85
  184.6 1.3 fusion.86
  190.0 1.3 fusion.86
  191.4 1.3 fusion.85
  192.7 1.3 fusion.86
  198.1 1.3 fusion.86
  199.5 1.3 fusion.85
  200.8 1.3 fusion.86
  206.2 1.3 fusion.86
  207.6 1.3 fusion.85
  208.9 1.3 fusion.86
  214.3 1.3 fusion.86
  215.7 1.3 fusion.85
  217.0 1.3 fusion.86
  218.4 3.9 convert_bitcast_fusion
  222.3 3.5 copy.93
  226.7 218.8 %reduce-scatter.2.cloned.1.call-done = bf16[1,8,1,16,768]{4,3,1,0,2:T(8,128)(2,1)} async-done(((bf16[32,8,1,16,768]{4,3,1,0,2:T(8,128)(2,1)}), bf16[1,8,1,16,768]{4,3,1,0,2:T(8,128)(2,1)}) %reduce-scatter.2.cloned.1.call-update) | async-done | bytes 196624 | tf_op jit(solution)/shard_map/reduce_scatter | solution.py:143
  445.4 9.4 %all-to-all-start.1 = ((bf16[8,1,16,768]{3,2,1,0:T(8,128)(2,1)}), bf16[8,1,16,768]{3,2,1,0:T(8,128)(2,1)S(1)}, u32[]{:S(2)}, u32[]{:S(2)}) async-start(bf16[8,1,16,768]{3,2,1,0:T(8,128)(2,1)} %bitcast.171), calls=%async_computation.2 | async-start | bytes 393216 | tf_op jit(solution)/shard_map/all_to_all | solution.py:146
  454.8 5.8 %all-to-all-done.1 = bf16[8,1,16,768]{3,2,1,0:T(8,128)(2,1)S(1)} async-done(((bf16[8,1,16,768]{3,2,1,0:T(8,128)(2,1)}), bf16[8,1,16,768]{3,2,1,0:T(8,128)(2,1)S(1)}, u32[]{:S(2)}, u32[]{:S(2)}) %all-to-all-start.1) | async-done | bytes 196640 | tf_op jit(solution)/shard_map/all_to_all | solution.py:146
  (87 shorter events, 44.8 us)
Async XLA Ops:
  7.2 3.4 copy-start
  7.2 5.8 %copy-start.6 = (bf16[16,2,128]{2,1,0:T(2,128)(2,1)S(1)}, bf16[16,2,128]{2,1,0:T(2,128)(2,1)}, u32[]{:S(2)}) copy-start(bf16[16,2,128]{2,1,0:T(2,128)(2,1)} %param.18) | copy-start | bytes 24580
  7.2 124.7 %all-gather.3.cloned.1.call-start = ((), (), s32[]{:S(2)}) async-start(), calls=%async_computation.4 | async-start | bytes 6488064 | tf_op jit(solution)/shard_map/all_gather | solution.py:120
  9.7 3.6 copy-start.5
  11.3 2.5 copy-start.4
  11.3 2.5 copy-start.1
  11.3 2.6 copy-start.2
  47.9 397.5 %reduce-scatter.2.cloned.1.call-start = ((), (), s32[]{:S(2)}) async-start(), calls=%async_computation.3 | async-start | bytes 6488064 | tf_op jit(solution)/shard_map/reduce_scatter | solution.py:143
  225.8 0.8 copy-start.3
  445.4 15.3 %all-to-all-start.1 = ((bf16[8,1,16,768]{3,2,1,0:T(8,128)(2,1)}), bf16[8,1,16,768]{3,2,1,0:T(8,128)(2,1)S(1)}, u32[]{:S(2)}, u32[]{:S(2)}) async-start(bf16[8,1,16,768]{3,2,1,0:T(8,128)(2,1)} %bitcast.171), calls=%async_computation.2 | async-start | bytes 393216 | tf_op jit(solution)/shard_map/all_to_all | solution.py:146
Sparse Core Ops, SparseCore 0:
  48.0 83.8 all-gather.2
  226.0 219.3 reduce-scatter.1
where the time goes:
time: 470 us; the launch traced here: 468 us
  waiting for transfers between devices  304 us (65%)
  matrix products  92.3 us (20%)
  blocking collectives  32 us (7%)
  between operations  14.3 us (3%)
  local copies, waits for them, and re-layouts  11.7 us (2%)
  starting transfers between devices  9.5 us (2%)
    reduce_scatter x1, waiting for transfers between devices, per_device(): lax.psum_scatter(down_terms.astype(jnp.bfloat16), ('grp', 'tp'), scatter_...  219 us
    all_gather x1, waiting for transfers between devices, per_device(): pieces = lax.all_gather(received, ('grp', 'tp'), axis=0, tiled=True)  79.5 us
    dot_general x32, matrix products, add_block(): jnp.einsum('ajcd,jdf->jacf', block, up_rows, preferred_element_type=jnp.f...  42.4 us
    dot_general x32, matrix products, add_block(): jnp.einsum('ajcd,jdf->jacf', block, gate_rows, preferred_element_type=jnp...  42.4 us
    psum x1, blocking collectives, per_device(): squares, logits = lax.psum((squares, partial_logits), 'tp')  17.7 us
    all_to_all x1, blocking collectives, per_device(): lax.all_to_all(outgoing, 'ex', split_axis=0, concat_axis=0, tiled=True)  14.3 us
    all_to_all x1, starting transfers between devices, per_device(): lax.all_to_all(summed[0].astype(jnp.bfloat16), 'ex', split_axis=0, concat...  9.42 us
  transfers between devices with their start and end apart: 3, of which 3 were waited for; matrix products, arithmetic and copies ran while one was open for 1% of the time, Pallas kernels for 0%

commit v1 on v0

--- a/solution.py
+++ b/solution.py
@@ -46,11 +46,6 @@
         "eskgt,etkd->eskgd", probs_fresh, values_now, preferred_element_type=jnp.float32
     )
     return heads_out.reshape(env_count, step_count, feature_count)
-
-
-def add_group(totals, addition, group_at):
-    current = lax.dynamic_slice_in_dim(totals, group_at, 1, 1)
-    return lax.dynamic_update_slice_in_dim(totals, current + addition[:, None], group_at, 1)
 
 
 def per_device(
@@ -107,7 +102,6 @@
         .reshape(row_count, topk, experts * CAP)
     )
     sender = jnp.sum(placed, axis=1)
-    gate_init = jnp.zeros((local_experts, group_count, owner_count, CAP, hidden_local), jnp.float32)
     packed = jnp.einsum(
         "rs,rd->sd",
         sender,
@@ -119,19 +113,15 @@
     received = received.reshape(1, owner_count, local_experts, CAP, slice_width)
     pieces = lax.all_gather(received, ("grp", "tp"), axis=0, tiled=True)
 
-    def add_block(position, running):
-        block = lax.dynamic_index_in_dim(pieces, position, 0, keepdims=False)
-        group_at = position // tensor_count
-        column_at = position % tensor_count
-        gate_rows = lax.dynamic_slice_in_dim(w_gate, column_at * slice_width, slice_width, 1)
-        up_rows = lax.dynamic_slice_in_dim(w_up, column_at * slice_width, slice_width, 1)
-        gate_add = jnp.einsum(
-            "ajcd,jdf->jacf", block, gate_rows, preferred_element_type=jnp.float32
-        )
-        up_add = jnp.einsum("ajcd,jdf->jacf", block, up_rows, preferred_element_type=jnp.float32)
-        return (add_group(running[0], gate_add, group_at), add_group(running[1], up_add, group_at))
-
-    gate_sums, up_sums = lax.fori_loop(0, pieces.shape[0], add_block, (gate_init, gate_init))
+    pieces = pieces.reshape(
+        group_count, tensor_count, owner_count, local_experts, CAP, slice_width
+    )
+    gate_split = w_gate.reshape(local_experts, tensor_count, slice_width, hidden_local)
+    up_split = w_up.reshape(local_experts, tensor_count, slice_width, hidden_local)
+    gate_sums = jnp.einsum(
+        "gtajcd,jtdf->jgacf", pieces, gate_split, preferred_element_type=jnp.float32
+    )
+    up_sums = jnp.einsum("gtajcd,jtdf->jgacf", pieces, up_split, preferred_element_type=jnp.float32)
     hidden = (jax.nn.silu(gate_sums) * up_sums).astype(jnp.bfloat16)
     down_split = w_down.reshape(local_experts, hidden_local, tensor_count, slice_width)
     down_terms = jnp.einsum(

time: 470 us -> 390 us (0.83)
  matrix products: 92.3 us -> 13.5 us
    dot_general x64 -> x2, matrix products: 84.8 us -> 6.5 us  [the longest x1 4.71 us: per_device(): jnp.einsum('gtajcd,jtdf->jgacf', pieces, gate_split, preferred_element_ty...]
where the time goes in v1:
time: 390 us; the launch traced here: 389 us
  waiting for transfers between devices  304 us (78%)
  blocking collectives  32 us (8%)
  between operations  14.3 us (4%)
  matrix products  13.5 us (3%)
  local copies, waits for them, and re-layouts  12.6 us (3%)
  starting transfers between devices  9.5 us (2%)
    reduce_scatter x1, waiting for transfers between devices, per_device(): lax.psum_scatter(down_terms.astype(jnp.bfloat16), ('grp', 'tp'), scatter_...  219 us
    all_gather x1, waiting for transfers between devices, per_device(): pieces = lax.all_gather(received, ('grp', 'tp'), axis=0, tiled=True)  79.5 us
    psum x1, blocking collectives, per_device(): squares, logits = lax.psum((squares, partial_logits), 'tp')  17.7 us
    all_to_all x1, blocking collectives, per_device(): lax.all_to_all(outgoing, 'ex', split_axis=0, concat_axis=0, tiled=True)  14.4 us
    all_to_all x1, starting transfers between devices, per_device(): lax.all_to_all(summed[0].astype(jnp.bfloat16), 'ex', split_axis=0, concat...  9.42 us
  transfers between devices with their start and end apart: 3, of which 3 were waited for; matrix products, arithmetic and copies ran while one was open for 1% of the time, Pallas kernels for 0%

profile of v1, /device:TPU:1, one launch (start us, length us, event | category | flops | bytes accessed | tf_op | source)
XLA Modules:
  0.0 389.3 jit_solution(13137319937710696107)
XLA Ops:
  7.2 0.0 copy-start
  7.2 0.0 all-gather.3.cloned.1.call-start
  7.2 0.8 broadcast_multiply_fusion
  8.1 0.8 copy.92
  8.9 0.8 reshape.262
  9.8 0.9 iota_compare_fusion.3
  10.6 2.3 fusion.55
  13.0 1.1 fusion.56
  14.2 0.3 fusion.28
  14.5 0.1 fusion.50
  14.6 0.3 fusion.46
  14.9 0.5 fusion.23
  15.4 0.1 reshape.261
  15.5 0.1 multiply_reduce_fusion
  15.6 0.5 fusion.37
  16.1 17.7 %all-reduce = (f32[16,2]{0,1:T(2,128)S(1)}, f32[16,2,8]{0,2,1:T(8,128)S(1)}) all-reduce(f32[16,2]{0,1:T(2,128)S(1)} %multiply_reduce_fusion, f32[16,2,8]{0,2,1:T(8,128)S(1)} %fusion.37), channel_id=1, replica_groups=mesh['grp'=4,'ex'=8,'tp'=8] {'tp'}, use_global_device_ids=true, to_apply=%region_6.7 | all-reduce | flops 288 | bytes 2304 | tf_op jit(solution)/shard_map/psum | solution.py:81
  33.8 0.1 divide_convert_fusion.2
  33.9 0.1 copy.91
  34.0 0.1 mul.92
  34.1 0.1 eq.68
  34.2 0.1 fusion.40
  34.3 0.1 reduce_window_sum.11
  34.4 0.2 select_reduce_fusion
  34.6 0.1 reduce_sum.64
  34.7 0.1 copy.93
  34.8 0.1 fusion.45
  34.8 0.1 copy.94
  34.9 0.2 convolution_convert_fusion
  35.2 14.4 %all_to_all.10 = bf16[8,16,768]{2,1,0:T(8,128)(2,1)} all-to-all(bf16[8,16,768]{2,1,0:T(8,128)(2,1)S(1)} %bitcast.164), channel_id=1, replica_groups=mesh['grp'=4,'ex'=8,'tp'=8] {'ex'}, dimensions={0} | all-to-all | bytes 393216 | tf_op jit(solution)/shard_map/all_to_all | solution.py:112
  49.5 0.0 all-gather.3.cloned.1.call-update
  49.5 0.0 reduce-scatter.2.cloned.1.call-start
  49.6 4.5 %copy.120 = bf16[32,8,8,768]{3,2,1,0:T(8,128)(2,1)} copy(bf16[32,8,8,768]{3,1,2,0:T(8,128)(2,1)} %bitcast.162) | data formatting | bytes 6291456
  54.1 79.5 %all-gather.3.cloned.1.call-done = bf16[256,16,768]{2,1,0:T(8,128)(2,1)} async-done(((bf16[8,16,768]{2,1,0:T(8,128)(2,1)}), bf16[256,16,768]{2,1,0:T(8,128)(2,1)}) %all-gather.3.cloned.1.call-update) | async-done | bytes 6291472 | tf_op jit(solution)/shard_map/all_gather | solution.py:114
  133.6 4.7 %convolution_bitcast_fusion.1 = f32[4,8,16,256]{3,2,1,0:T(8,128)S(1)} fusion(bf16[4,8,8,16,768]{4,3,2,1,0:T(8,128)(2,1)} %bitcast.168, bf16[8,768,256,1,1]{2,1,4,0,3:T(8,128)(2,1)S(1)} %bitcast.159), kind=kOutput, calls=%fused_computation.8 | convolution fusion | flops 1610612736 | bytes 9961472 | tf_op jit(solution)/shard_map/gtajcd,jtdf->jgacf/dot_general | solution.py:121
  138.3 0.8 copy-done.7
  139.1 1.8 fusion.19
  140.9 0.1 copy-done.1
  141.0 1.9 convert_bitcast_fusion
  142.9 3.5 copy.98
  146.5 0.0 reduce-scatter.2.cloned.1.call-update
  146.5 0.7 copy.102
  147.2 0.1 iota_compare_fusion.1
  147.3 219.0 %reduce-scatter.2.cloned.1.call-done = bf16[1,8,1,16,768]{4,3,1,0,2:T(8,128)(2,1)} async-done(((bf16[32,8,1,16,768]{4,3,1,0,2:T(8,128)(2,1)}), bf16[1,8,1,16,768]{4,3,1,0,2:T(8,128)(2,1)}) %reduce-scatter.2.cloned.1.call-update) | async-done | bytes 196624 | tf_op jit(solution)/shard_map/reduce_scatter | solution.py:133
  366.3 9.4 %all-to-all-start.1 = ((bf16[8,1,16,768]{3,2,1,0:T(8,128)(2,1)}), bf16[8,1,16,768]{3,2,1,0:T(8,128)(2,1)S(1)}, u32[]{:S(2)}, u32[]{:S(2)}) async-start(bf16[8,1,16,768]{3,2,1,0:T(8,128)(2,1)} %bitcast.165), calls=%async_computation.2 | async-start | bytes 393216 | tf_op jit(solution)/shard_map/all_to_all | solution.py:136
  375.7 5.8 %all-to-all-done.1 = bf16[8,1,16,768]{3,2,1,0:T(8,128)(2,1)S(1)} async-done(((bf16[8,1,16,768]{3,2,1,0:T(8,128)(2,1)}), bf16[8,1,16,768]{3,2,1,0:T(8,128)(2,1)S(1)}, u32[]{:S(2)}, u32[]{:S(2)}) %all-to-all-start.1) | async-done | bytes 196640 | tf_op jit(solution)/shard_map/all_to_all | solution.py:136
  381.6 0.2 fusion.42
  381.7 0.1 fusion.35
  381.8 0.7 copy.103
  (28 shorter events, 0.2 us)
Async XLA Ops:
  7.2 126.4 %copy-start = (bf16[1,6144,256]{2,1,0:T(8,128)(2,1)S(1)}, bf16[1,6144,256]{2,1,0:T(8,128)(2,1)}, u32[]{:S(2)}) copy-start(bf16[1,6144,256]{2,1,0:T(8,128)(2,1)} %param.23) | copy-start | bytes 9437188
  7.2 7.4 %copy-start.9 = (bf16[16,2,128]{2,1,0:T(2,128)(2,1)S(1)}, bf16[16,2,128]{2,1,0:T(2,128)(2,1)}, u32[]{:S(2)}) copy-start(bf16[16,2,128]{2,1,0:T(2,128)(2,1)} %param.16) | copy-start | bytes 24580
  7.2 126.4 %all-gather.3.cloned.1.call-start = ((), (), s32[]{:S(2)}) async-start(), calls=%async_computation.4 | async-start | bytes 6488064 | tf_op jit(solution)/shard_map/all_gather | solution.py:114
  9.8 5.2 %copy-start.8 = (bf16[16,1,512,128]{3,2,1,0:T(8,128)(2,1)S(1)}, bf16[16,1,512,128]{3,2,1,0:T(8,128)(2,1)}, u32[]{:S(2)}) copy-start(bf16[16,1,512,128]{3,2,1,0:T(8,128)(2,1)} %param.18) | copy-start | bytes 6291460
  13.0 2.5 copy-start.5
  13.0 2.5 copy-start.2
  13.0 2.6 copy-start.3
  49.5 316.7 %reduce-scatter.2.cloned.1.call-start = ((), (), s32[]{:S(2)}) async-start(), calls=%async_computation.3 | async-start | bytes 6488064 | tf_op jit(solution)/shard_map/reduce_scatter | solution.py:133
  133.6 4.7 %copy-start.6 = (bf16[256,16,768]{2,1,0:T(8,128)(2,1)S(1)}, bf16[256,16,768]{2,1,0:T(8,128)(2,1)}, u32[]{:S(2)}) copy-start(bf16[256,16,768]{2,1,0:T(8,128)(2,1)} %all-gather.3.cloned.1.call-done) | copy-start | bytes 18874372
  133.6 5.5 %copy-start.7 = (bf16[1,6144,256]{2,1,0:T(8,128)(2,1)S(1)}, bf16[1,6144,256]{2,1,0:T(8,128)(2,1)}, u32[]{:S(2)}) copy-start(bf16[1,6144,256]{2,1,0:T(8,128)(2,1)} %param.24) | copy-start | bytes 9437188
  139.1 1.9 copy-start.1
  146.5 0.8 copy-start.4
  366.3 15.3 %all-to-all-start.1 = ((bf16[8,1,16,768]{3,2,1,0:T(8,128)(2,1)}), bf16[8,1,16,768]{3,2,1,0:T(8,128)(2,1)S(1)}, u32[]{:S(2)}, u32[]{:S(2)}) async-start(bf16[8,1,16,768]{3,2,1,0:T(8,128)(2,1)} %bitcast.165), calls=%async_computation.2 | async-start | bytes 393216 | tf_op jit(solution)/shard_map/all_to_all | solution.py:136
Sparse Core Ops, SparseCore 0:
  49.7 83.8 all-gather.2
  146.6 219.6 reduce-scatter.1

commit v2 on v1

--- a/solution.py
+++ b/solution.py
@@ -46,6 +46,21 @@
         "eskgt,etkd->eskgd", probs_fresh, values_now, preferred_element_type=jnp.float32
     )
     return heads_out.reshape(env_count, step_count, feature_count)
+
+
+def ring_reduce_scatter(parts, axis, count, direction):
+    me = lax.axis_index(axis)
+    pairs = [(j, (j + direction) % count) for j in range(count)]
+
+    def own(offset):
+        chunk = (me - direction * offset) % count
+        return lax.dynamic_index_in_dim(parts, chunk, 0, keepdims=False)
+
+    total = own(1)
+    for step in range(count - 1):
+        arrived = lax.ppermute(total.astype(jnp.bfloat16), axis, pairs)
+        total = arrived.astype(jnp.float32) + own(step + 2)
+    return total
 
 
 def per_device(
@@ -125,14 +140,14 @@
     hidden = (jax.nn.silu(gate_sums) * up_sums).astype(jnp.bfloat16)
     down_split = w_down.reshape(local_experts, hidden_local, tensor_count, slice_width)
     down_terms = jnp.einsum(
-        "jgacf,jftd->gtajcd", hidden, down_split, preferred_element_type=jnp.float32
+        "jgacf,jftd->tgajcd", hidden, down_split, preferred_element_type=jnp.float32
     )
-    down_terms = down_terms.reshape(
-        group_count * tensor_count, owner_count, local_experts, CAP, slice_width
-    )
-    summed = lax.psum_scatter(
-        down_terms.astype(jnp.bfloat16), ("grp", "tp"), scatter_dimension=0, tiled=True
-    ).astype(jnp.float32)
+    half = group_count // 2
+    clockwise = ring_reduce_scatter(down_terms[:, :half], "tp", tensor_count, 1)
+    counter = ring_reduce_scatter(down_terms[:, half:], "tp", tensor_count, -1)
+    over_tp = jnp.concatenate([clockwise, counter], axis=0).astype(jnp.bfloat16)
+    summed = lax.psum_scatter(over_tp, "grp", scatter_dimension=0, tiled=True)
+    summed = summed.astype(jnp.float32)
     returned = lax.all_to_all(
         summed[0].astype(jnp.bfloat16), "ex", split_axis=0, concat_axis=0, tiled=True
     )

time: 390 us -> 295 us (0.76)
  waiting for transfers between devices: 304 us -> 155 us
  other arithmetic: 2.98 us -> 28 us
  local copies, waits for them, and re-layouts: 12.6 us -> 24.1 us
  starting transfers between devices: 9.5 us -> 20.1 us
  matrix products: 13.5 us -> 20.4 us
    reduce_scatter x1, waiting for transfers between devices: 219 us -> 28.2 us  [per_device(): summed = lax.psum_scatter(over_tp, 'grp', scatter_dimension=0, tiled=True)]
    ppermute x0 -> x14, waiting for transfers between devices: none -> 41.3 us  [ring_reduce_scatter(): arrived = lax.ppermute(total.astype(jnp.bfloat16), axis, pairs)]
    convert_element_type x0 -> x12, other arithmetic: none -> 20.4 us  [ring_reduce_scatter(): arrived = lax.ppermute(total.astype(jnp.bfloat16), axis, pairs)]
    ppermute x0 -> x14, starting transfers between devices: none -> 12.9 us  [ring_reduce_scatter(): arrived = lax.ppermute(total.astype(jnp.bfloat16), axis, pairs)]
    slice x0 -> x1, local copies, waits for them, and re-layouts: none -> 11.1 us  [per_device(): clockwise = ring_reduce_scatter(down_terms[:, :half], 'tp', tensor_count, 1)]
    dot_general x1, matrix products: 1.92 us -> 6.47 us  [per_device(): jnp.einsum('jgacf,jftd->tgajcd', hidden, down_split, preferred_element_ty...]
    unnamed x24 -> x22, local copies, waits for them, and re-layouts: 7.58 us -> 8.42 us
  transfers between devices with their start and end apart: 3 -> 17, of which waited for: 3 -> 17; matrix products, arithmetic and copies ran while one was open for 1% -> 10% of each run, Pallas kernels for 0% -> 0%
where the time goes in v2:
time: 295 us; the launch traced here: 294 us
  waiting for transfers between devices  155 us (53%)
  blocking collectives  32.6 us (11%)
  other arithmetic  28 us (9%)
  local copies, waits for them, and re-layouts  24.1 us (8%)
  matrix products  20.4 us (7%)
  starting transfers between devices  20.1 us (7%)
  between operations  14.3 us (5%)
    all_gather x1, waiting for transfers between devices, per_device(): pieces = lax.all_gather(received, ('grp', 'tp'), axis=0, tiled=True)  79.4 us
    ppermute x14, waiting for transfers between devices, ring_reduce_scatter(): arrived = lax.ppermute(total.astype(jnp.bfloat16), axis, pairs)  41.3 us
    reduce_scatter x1, waiting for transfers between devices, per_device(): summed = lax.psum_scatter(over_tp, 'grp', scatter_dimension=0, tiled=True)  28.2 us
    convert_element_type x12, other arithmetic, ring_reduce_scatter(): arrived = lax.ppermute(total.astype(jnp.bfloat16), axis, pairs)  20.4 us
    psum x1, blocking collectives, per_device(): squares, logits = lax.psum((squares, partial_logits), 'tp')  18.3 us
    all_to_all x1, blocking collectives, per_device(): lax.all_to_all(outgoing, 'ex', split_axis=0, concat_axis=0, tiled=True)  14.3 us
    ppermute x14, starting transfers between devices, ring_reduce_scatter(): arrived = lax.ppermute(total.astype(jnp.bfloat16), axis, pairs)  12.9 us
    slice x1, local copies, waits for them, and re-layouts, per_device(): clockwise = ring_reduce_scatter(down_terms[:, :half], 'tp', tensor_count, 1)  11.1 us
  transfers between devices with their start and end apart: 17, of which 17 were waited for; matrix products, arithmetic and copies ran while one was open for 10% of the time, Pallas kernels for 0%

profile of v2, /device:TPU:1, one launch (start us, length us, event | category | flops | bytes accessed | tf_op | source)
XLA Modules:
  0.0 294.5 jit_solution(10479550490367904286)
XLA Ops:
  10.5 2.3 fusion.72
  12.9 1.1 fusion.73
  15.4 2.1 fusion.23
  18.2 18.3 %all-reduce = (f32[16,2]{0,1:T(2,128)S(1)}, f32[16,2,8]{0,2,1:T(8,128)}) all-reduce(f32[16,2]{0,1:T(2,128)S(1)} %multiply_reduce_fusion, f32[16,2,8]{0,2,1:T(8,128)S(1)} %fusion.53), channel_id=1, replica_groups=mesh['grp'=4,'ex'=8,'tp'=8] {'tp'}, use_global_device_ids=true, to_apply=%region_6.7 | all-reduce | flops 288 | bytes 2304 | tf_op jit(solution)/shard_map/psum | solution.py:96
  38.4 14.3 %all_to_all.10 = bf16[8,16,768]{2,1,0:T(8,128)(2,1)} all-to-all(bf16[8,16,768]{2,1,0:T(8,128)(2,1)S(1)} %bitcast.240), channel_id=1, replica_groups=mesh['grp'=4,'ex'=8,'tp'=8] {'ex'}, dimensions={0} | all-to-all | bytes 393216 | tf_op jit(solution)/shard_map/all_to_all | solution.py:127
  52.8 4.5 %copy.130 = bf16[32,8,8,768]{3,2,1,0:T(8,128)(2,1)} copy(bf16[32,8,8,768]{3,1,2,0:T(8,128)(2,1)} %bitcast.238) | data formatting | bytes 6291456
  57.3 79.4 %all-gather.3.cloned.1.call-done = bf16[256,16,768]{2,1,0:T(8,128)(2,1)} async-done(((bf16[8,16,768]{2,1,0:T(8,128)(2,1)}), bf16[256,16,768]{2,1,0:T(8,128)(2,1)}) %all-gather.3.cloned.1.call-update) | async-done | bytes 6291472 | tf_op jit(solution)/shard_map/all_gather | solution.py:129
  136.7 4.7 %convolution_bitcast_fusion.2 = f32[4,8,16,256]{3,2,1,0:T(8,128)S(1)} fusion(bf16[4,8,8,16,768]{4,3,2,1,0:T(8,128)(2,1)} %bitcast.244, bf16[8,768,256,1,1]{2,1,4,0,3:T(8,128)(2,1)S(1)} %bitcast.236), kind=kOutput, calls=%fused_computation.8 | convolution fusion | flops 1610612736 | bytes 9961472 | tf_op jit(solution)/shard_map/gtajcd,jtdf->jgacf/dot_general | solution.py:136
  142.3 1.8 fusion.19
  144.2 6.5 %convolution_bitcast_fusion = f32[8,4,8,1,16,768]{5,4,0,2,1,3:T(8,128)} fusion(bf16[4,8,16,256,1]{3,2,4,1,0:T(8,128)(2,1)S(1)} %fusion.19, bf16[256,8,768,1,1]{2,1,0,4,3:T(8,128)(2,1)S(1)} %bitcast.237), kind=kOutput, calls=%fused_computation | convolution fusion | flops 1610612736 | bytes 15990784 | tf_op jit(solution)/shard_map/jgacf,jftd->tgajcd/dot_general | solution.py:142
  150.7 11.1 %fusion.71 = (f32[8,2,8,1,16,768]{5,4,0,2,1,3:T(8,128)}, f32[8,2,8,1,16,768]{5,4,0,2,1,3:T(8,128)}) fusion(f32[8,4,8,1,16,768]{5,4,0,2,1,3:T(8,128)} %convolution_bitcast_fusion), kind=kLoop, calls=%fused_computation.104 | loop fusion | bytes 25165824 | tf_op jit(solution)/shard_map/slice | solution.py:146
  161.8 1.2 fusion.43
  162.9 1.2 collective-permute-start.7
  164.1 1.9 fusion.44
  166.4 5.8 %collective-permute-done.7 = bf16[2,8,1,16,768]{4,3,1,0,2:T(8,128)(2,1)} collective-permute-done((bf16[2,8,1,16,768]{4,3,1,0,2:T(8,128)(2,1)S(1)}, bf16[2,8,1,16,768]{4,3,1,0,2:T(8,128)(2,1)}, u32[]{:S(2)}, u32[]{:S(2)}) %collective-permute-start.7) | collective-permute-done | bytes 393248 | tf_op jit(solution)/shard_map/ppermute | solution.py:61
  172.2 1.3 fusion.41
  173.5 2.0 collective-permute-start.8
  175.9 2.1 fusion.34
  177.9 4.2 %collective-permute-done.8 = bf16[2,8,1,16,768]{4,3,1,0,2:T(8,128)(2,1)} collective-permute-done((bf16[2,8,1,16,768]{4,3,1,0,2:T(8,128)(2,1)S(1)}, bf16[2,8,1,16,768]{4,3,1,0,2:T(8,128)(2,1)}, u32[]{:S(2)}, u32[]{:S(2)}) %collective-permute-start.8) | collective-permute-done | bytes 393248 | tf_op jit(solution)/shard_map/ppermute | solution.py:61
  182.1 1.3 fusion.40
  183.4 2.6 collective-permute-start.9
  186.9 2.1 fusion.33
  189.0 2.0 collective-permute-done.9
  191.0 1.3 fusion.39
  192.3 3.0 %collective-permute-start.10 = (bf16[2,8,1,16,768]{4,3,1,0,2:T(8,128)(2,1)S(1)}, bf16[2,8,1,16,768]{4,3,1,0,2:T(8,128)(2,1)}, u32[]{:S(2)}, u32[]{:S(2)}) collective-permute-start(bf16[2,8,1,16,768]{4,3,1,0,2:T(8,128)(2,1)S(1)} %fusion.39), channel_id=1, source_target_pairs={{0,7},{1,0},{2,1},{3,2},{4,3},{5,4},{6,5},{7,6},{8,15},{9,8},{10,9... | collective-permute-start | bytes 1179656 | tf_op jit(solution)/shard_map/ppermute | solution.py:61
  195.3 1.8 collective-permute-done.2
  197.1 2.1 fusion.32
  199.2 4.1 %collective-permute-done.10 = bf16[2,8,1,16,768]{4,3,1,0,2:T(8,128)(2,1)} collective-permute-done((bf16[2,8,1,16,768]{4,3,1,0,2:T(8,128)(2,1)S(1)}, bf16[2,8,1,16,768]{4,3,1,0,2:T(8,128)(2,1)}, u32[]{:S(2)}, u32[]{:S(2)}) %collective-permute-start.10) | collective-permute-done | bytes 393248 | tf_op jit(solution)/shard_map/ppermute | solution.py:61
  203.3 1.3 fusion.38
  204.7 2.6 collective-permute-done.3
  207.4 2.1 fusion.31
  209.4 2.8 collective-permute-done.11
  212.2 1.3 fusion.37
  214.3 3.3 %collective-permute-done.4 = bf16[2,8,1,16,768]{4,3,1,0,2:T(8,128)(2,1)} collective-permute-done((bf16[2,8,1,16,768]{4,3,1,0,2:T(8,128)(2,1)}, bf16[2,8,1,16,768]{4,3,1,0,2:T(8,128)(2,1)}, u32[]{:S(2)}, u32[]{:S(2)}) %collective-permute-start.4) | collective-permute-done | bytes 393248 | tf_op jit(solution)/shard_map/ppermute | solution.py:61
  217.6 2.1 fusion.30
  219.7 1.2 collective-permute-done.12
  220.9 1.3 fusion.36
  222.2 2.9 collective-permute-start.13
  225.1 3.6 %collective-permute-done.5 = bf16[2,8,1,16,768]{4,3,1,0,2:T(8,128)(2,1)} collective-permute-done((bf16[2,8,1,16,768]{4,3,1,0,2:T(8,128)(2,1)}, bf16[2,8,1,16,768]{4,3,1,0,2:T(8,128)(2,1)}, u32[]{:S(2)}, u32[]{:S(2)}) %collective-permute-start.5) | collective-permute-done | bytes 393248 | tf_op jit(solution)/shard_map/ppermute | solution.py:61
  228.7 2.1 fusion.29
  230.8 1.6 collective-permute-done.13
  232.3 1.3 fusion.35
  233.7 7.2 %collective-permute-done.6 = bf16[2,8,1,16,768]{4,3,1,0,2:T(8,128)(2,1)} collective-permute-done((bf16[2,8,1,16,768]{4,3,1,0,2:T(8,128)(2,1)}, bf16[2,8,1,16,768]{4,3,1,0,2:T(8,128)(2,1)}, u32[]{:S(2)}, u32[]{:S(2)}) %collective-permute-start.6) | collective-permute-done | bytes 393248 | tf_op jit(solution)/shard_map/ppermute | solution.py:61
  240.9 1.3 fusion.28
  243.2 1.5 copy.103
  245.5 28.2 %reduce-scatter.2.cloned.1.call-done = bf16[1,8,1,16,768]{4,3,1,0,2:T(8,128)(2,1)} async-done(((bf16[4,8,1,16,768]{4,3,1,0,2:T(8,128)(2,1)}), bf16[1,8,1,16,768]{4,3,1,0,2:T(8,128)(2,1)}) %reduce-scatter.2.cloned.1.call-update) | async-done | bytes 196624 | tf_op jit(solution)/shard_map/reduce_scatter | solution.py:149
  273.7 7.1 %all-to-all-start.1 = ((bf16[8,1,16,768]{3,2,1,0:T(8,128)(2,1)}), bf16[8,1,16,768]{3,2,1,0:T(8,128)(2,1)S(1)}, u32[]{:S(2)}, u32[]{:S(2)}) async-start(bf16[8,1,16,768]{3,2,1,0:T(8,128)(2,1)} %bitcast.241), calls=%async_computation.2 | async-start | bytes 393216 | tf_op jit(solution)/shard_map/all_to_all | solution.py:151
  280.8 5.8 %all-to-all-done.1 = bf16[8,1,16,768]{3,2,1,0:T(8,128)(2,1)S(1)} async-done(((bf16[8,1,16,768]{3,2,1,0:T(8,128)(2,1)}), bf16[8,1,16,768]{3,2,1,0:T(8,128)(2,1)S(1)}, u32[]{:S(2)}, u32[]{:S(2)}) %all-to-all-start.1) | async-done | bytes 196640 | tf_op jit(solution)/shard_map/all_to_all | solution.py:151
  (72 shorter events, 13.4 us)
Async XLA Ops:
  7.2 129.6 %copy-start = (bf16[1,6144,256]{2,1,0:T(8,128)(2,1)S(1)}, bf16[1,6144,256]{2,1,0:T(8,128)(2,1)}, u32[]{:S(2)}) copy-start(bf16[1,6144,256]{2,1,0:T(8,128)(2,1)} %param.23) | copy-start | bytes 9437188
  7.2 10.4 %copy-start.5 = (bf16[768]{0:T(1024)(128)(2,1)S(1)}, bf16[768]{0:T(1024)(128)(2,1)}, u32[]{:S(2)}) copy-start(bf16[768]{0:T(1024)(128)(2,1)} %param.20) | copy-start | bytes 4612
  7.2 10.4 %copy-start.2 = (bf16[16,2,768]{2,1,0:T(2,128)(2,1)S(1)}, bf16[16,2,768]{2,1,0:T(2,128)(2,1)}, u32[]{:S(2)}) copy-start(bf16[16,2,768]{2,1,0:T(2,128)(2,1)} %param.13) | copy-start | bytes 147460
  7.2 10.5 %copy-start.3 = (f32[768,8]{0,1:T(8,128)S(1)}, f32[768,8]{0,1:T(8,128)}, u32[]{:S(2)}) copy-start(f32[768,8]{0,1:T(8,128)} %param.21) | copy-start | bytes 73732
  7.2 129.5 %all-gather.3.cloned.1.call-start = ((), (), s32[]{:S(2)}) async-start(), calls=%async_computation.4 | async-start | bytes 6488064 | tf_op jit(solution)/shard_map/all_gather | solution.py:129
  52.7 221.0 %reduce-scatter.2.cloned.1.call-start = ((), (), s32[]{:S(2)}) async-start(), calls=%async_computation.3 | async-start | bytes 983040 | tf_op jit(solution)/shard_map/reduce_scatter | solution.py:149
  136.7 4.7 %slice-start = ((s8[6291456]{0:T(1024)(128)(4,1)}), s8[4194304]{0:T(1024)(128)(4,1)S(1)}, s32[]{:S(2)}) async-start(s8[6291456]{0:T(1024)(128)(4,1)} %bitcast.245), calls=%async_computation.5 | async-start | bytes 8388608
  136.7 5.0 %copy-start.6 = (bf16[1,6144,256]{2,1,0:T(8,128)(2,1)S(1)}, bf16[1,6144,256]{2,1,0:T(8,128)(2,1)}, u32[]{:S(2)}) copy-start(bf16[1,6144,256]{2,1,0:T(8,128)(2,1)} %param.24) | copy-start | bytes 9437188
  136.7 5.6 %slice-start.1 = ((s8[6291456]{0:T(1024)(128)(4,1)}), s8[2097152]{0:T(1024)(128)(4,1)S(1)}, s32[]{:S(2)}) async-start(s8[6291456]{0:T(1024)(128)(4,1)} %bitcast.245), calls=%async_computation.6 | async-start | bytes 4194304
  142.3 1.9 copy-start.1
  162.9 9.2 %collective-permute-start.7 = (bf16[2,8,1,16,768]{4,3,1,0,2:T(8,128)(2,1)S(1)}, bf16[2,8,1,16,768]{4,3,1,0,2:T(8,128)(2,1)}, u32[]{:S(2)}, u32[]{:S(2)}) collective-permute-start(bf16[2,8,1,16,768]{4,3,1,0,2:T(8,128)(2,1)S(1)} %fusion.43), channel_id=1, source_target_pairs={{0,7},{1,0},{2,1},{3,2},{4,3},{5,4},{6,5},{7,6},{8,15},{9,8},{10,9... | collective-permute-start | bytes 1179656 | tf_op jit(solution)/shard_map/ppermute | solution.py:61
  166.1 9.8 %collective-permute-start = (bf16[2,8,1,16,768]{4,3,1,0,2:T(8,128)(2,1)}, bf16[2,8,1,16,768]{4,3,1,0,2:T(8,128)(2,1)}, u32[]{:S(2)}, u32[]{:S(2)}) collective-permute-start(bf16[2,8,1,16,768]{4,3,1,0,2:T(8,128)(2,1)} %fusion.44), channel_id=1, source_target_pairs={{0,1},{1,2},{2,3},{3,4},{4,5},{5,6},{6,7},{7,0},{8,9},{9,10},{10,1... | collective-permute-start | bytes 1179656 | tf_op jit(solution)/shard_map/ppermute | solution.py:61
  173.5 8.6 %collective-permute-start.8 = (bf16[2,8,1,16,768]{4,3,1,0,2:T(8,128)(2,1)S(1)}, bf16[2,8,1,16,768]{4,3,1,0,2:T(8,128)(2,1)}, u32[]{:S(2)}, u32[]{:S(2)}) collective-permute-start(bf16[2,8,1,16,768]{4,3,1,0,2:T(8,128)(2,1)S(1)} %fusion.41), channel_id=1, source_target_pairs={{0,7},{1,0},{2,1},{3,2},{4,3},{5,4},{6,5},{7,6},{8,15},{9,8},{10,9... | collective-permute-start | bytes 1179656 | tf_op jit(solution)/shard_map/ppermute | solution.py:61
  177.9 8.9 %collective-permute-start.1 = (bf16[2,8,1,16,768]{4,3,1,0,2:T(8,128)(2,1)}, bf16[2,8,1,16,768]{4,3,1,0,2:T(8,128)(2,1)}, u32[]{:S(2)}, u32[]{:S(2)}) collective-permute-start(bf16[2,8,1,16,768]{4,3,1,0,2:T(8,128)(2,1)} %fusion.34), channel_id=1, source_target_pairs={{0,1},{1,2},{2,3},{3,4},{4,5},{5,6},{6,7},{7,0},{8,9},{9,10},{10,1... | collective-permute-start | bytes 1179656 | tf_op jit(solution)/shard_map/ppermute | solution.py:61
  183.4 7.5 %collective-permute-start.9 = (bf16[2,8,1,16,768]{4,3,1,0,2:T(8,128)(2,1)S(1)}, bf16[2,8,1,16,768]{4,3,1,0,2:T(8,128)(2,1)}, u32[]{:S(2)}, u32[]{:S(2)}) collective-permute-start(bf16[2,8,1,16,768]{4,3,1,0,2:T(8,128)(2,1)S(1)} %fusion.40), channel_id=1, source_target_pairs={{0,7},{1,0},{2,1},{3,2},{4,3},{5,4},{6,5},{7,6},{8,15},{9,8},{10,9... | collective-permute-start | bytes 1179656 | tf_op jit(solution)/shard_map/ppermute | solution.py:61
  189.0 8.2 %collective-permute-start.2 = (bf16[2,8,1,16,768]{4,3,1,0,2:T(8,128)(2,1)}, bf16[2,8,1,16,768]{4,3,1,0,2:T(8,128)(2,1)}, u32[]{:S(2)}, u32[]{:S(2)}) collective-permute-start(bf16[2,8,1,16,768]{4,3,1,0,2:T(8,128)(2,1)} %fusion.33), channel_id=1, source_target_pairs={{0,1},{1,2},{2,3},{3,4},{4,5},{5,6},{6,7},{7,0},{8,9},{9,10},{10,1... | collective-permute-start | bytes 1179656 | tf_op jit(solution)/shard_map/ppermute | solution.py:61
  192.3 11.0 %collective-permute-start.10 = (bf16[2,8,1,16,768]{4,3,1,0,2:T(8,128)(2,1)S(1)}, bf16[2,8,1,16,768]{4,3,1,0,2:T(8,128)(2,1)}, u32[]{:S(2)}, u32[]{:S(2)}) collective-permute-start(bf16[2,8,1,16,768]{4,3,1,0,2:T(8,128)(2,1)S(1)} %fusion.39), channel_id=1, source_target_pairs={{0,7},{1,0},{2,1},{3,2},{4,3},{5,4},{6,5},{7,6},{8,15},{9,8},{10,9... | collective-permute-start | bytes 1179656 | tf_op jit(solution)/shard_map/ppermute | solution.py:61
  199.2 8.2 %collective-permute-start.3 = (bf16[2,8,1,16,768]{4,3,1,0,2:T(8,128)(2,1)}, bf16[2,8,1,16,768]{4,3,1,0,2:T(8,128)(2,1)}, u32[]{:S(2)}, u32[]{:S(2)}) collective-permute-start(bf16[2,8,1,16,768]{4,3,1,0,2:T(8,128)(2,1)} %fusion.32), channel_id=1, source_target_pairs={{0,1},{1,2},{2,3},{3,4},{4,5},{5,6},{6,7},{7,0},{8,9},{9,10},{10,1... | collective-permute-start | bytes 1179656 | tf_op jit(solution)/shard_map/ppermute | solution.py:61
  204.6 7.6 %collective-permute-start.11 = (bf16[2,8,1,16,768]{4,3,1,0,2:T(8,128)(2,1)S(1)}, bf16[2,8,1,16,768]{4,3,1,0,2:T(8,128)(2,1)}, u32[]{:S(2)}, u32[]{:S(2)}) collective-permute-start(bf16[2,8,1,16,768]{4,3,1,0,2:T(8,128)(2,1)S(1)} %fusion.38), channel_id=1, source_target_pairs={{0,7},{1,0},{2,1},{3,2},{4,3},{5,4},{6,5},{7,6},{8,15},{9,8},{10,9... | collective-permute-start | bytes 1179656 | tf_op jit(solution)/shard_map/ppermute | solution.py:61
  209.4 36.0 %copy-start.4 = (s32[16,2,2]{0,2,1:T(2,128)S(1)}, s32[16,2,2]{0,2,1:T(2,128)}, u32[]{:S(2)}) copy-start(s32[16,2,2]{0,2,1:T(2,128)} %param.22) | copy-start | bytes 772
  209.4 8.2 %collective-permute-start.4 = (bf16[2,8,1,16,768]{4,3,1,0,2:T(8,128)(2,1)}, bf16[2,8,1,16,768]{4,3,1,0,2:T(8,128)(2,1)}, u32[]{:S(2)}, u32[]{:S(2)}) collective-permute-start(bf16[2,8,1,16,768]{4,3,1,0,2:T(8,128)(2,1)} %fusion.31), channel_id=1, source_target_pairs={{0,1},{1,2},{2,3},{3,4},{4,5},{5,6},{6,7},{7,0},{8,9},{9,10},{10,1... | collective-permute-start | bytes 1179656 | tf_op jit(solution)/shard_map/ppermute | solution.py:61
  213.5 7.3 %collective-permute-start.12 = (bf16[2,8,1,16,768]{4,3,1,0,2:T(8,128)(2,1)S(1)}, bf16[2,8,1,16,768]{4,3,1,0,2:T(8,128)(2,1)}, u32[]{:S(2)}, u32[]{:S(2)}) collective-permute-start(bf16[2,8,1,16,768]{4,3,1,0,2:T(8,128)(2,1)S(1)} %fusion.37), channel_id=1, source_target_pairs={{0,7},{1,0},{2,1},{3,2},{4,3},{5,4},{6,5},{7,6},{8,15},{9,8},{10,9... | collective-permute-start | bytes 1179656 | tf_op jit(solution)/shard_map/ppermute | solution.py:61
  219.7 9.0 %collective-permute-start.5 = (bf16[2,8,1,16,768]{4,3,1,0,2:T(8,128)(2,1)}, bf16[2,8,1,16,768]{4,3,1,0,2:T(8,128)(2,1)}, u32[]{:S(2)}, u32[]{:S(2)}) collective-permute-start(bf16[2,8,1,16,768]{4,3,1,0,2:T(8,128)(2,1)} %fusion.30), channel_id=1, source_target_pairs={{0,1},{1,2},{2,3},{3,4},{4,5},{5,6},{6,7},{7,0},{8,9},{9,10},{10,1... | collective-permute-start | bytes 1179656 | tf_op jit(solution)/shard_map/ppermute | solution.py:61
  222.2 10.2 %collective-permute-start.13 = (bf16[2,8,1,16,768]{4,3,1,0,2:T(8,128)(2,1)S(1)}, bf16[2,8,1,16,768]{4,3,1,0,2:T(8,128)(2,1)}, u32[]{:S(2)}, u32[]{:S(2)}) collective-permute-start(bf16[2,8,1,16,768]{4,3,1,0,2:T(8,128)(2,1)S(1)} %fusion.36), channel_id=1, source_target_pairs={{0,7},{1,0},{2,1},{3,2},{4,3},{5,4},{6,5},{7,6},{8,15},{9,8},{10,9... | collective-permute-start | bytes 1179656 | tf_op jit(solution)/shard_map/ppermute | solution.py:61
  230.8 10.1 %collective-permute-start.6 = (bf16[2,8,1,16,768]{4,3,1,0,2:T(8,128)(2,1)}, bf16[2,8,1,16,768]{4,3,1,0,2:T(8,128)(2,1)}, u32[]{:S(2)}, u32[]{:S(2)}) collective-permute-start(bf16[2,8,1,16,768]{4,3,1,0,2:T(8,128)(2,1)} %fusion.29), channel_id=1, source_target_pairs={{0,1},{1,2},{2,3},{3,4},{4,5},{5,6},{6,7},{7,0},{8,9},{9,10},{10,1... | collective-permute-start | bytes 1179656 | tf_op jit(solution)/shard_map/ppermute | solution.py:61
  273.7 13.0 %all-to-all-start.1 = ((bf16[8,1,16,768]{3,2,1,0:T(8,128)(2,1)}), bf16[8,1,16,768]{3,2,1,0:T(8,128)(2,1)S(1)}, u32[]{:S(2)}, u32[]{:S(2)}) async-start(bf16[8,1,16,768]{3,2,1,0:T(8,128)(2,1)} %bitcast.241), calls=%async_computation.2 | async-start | bytes 393216 | tf_op jit(solution)/shard_map/all_to_all | solution.py:151
Sparse Core Ops, SparseCore 0:
  52.9 83.8 all-gather.2
  243.3 30.3 reduce-scatter.1
